TPU v7x, 256 devices: a whole 4x4x8 slice. The times are simulated.
256 devices in a mesh: dp: 4 (over y), expert: 64 (over z, x, core).
Axes of the slice: x: 4, y: 4, z: 8, core: 2. Of those that a mesh axis runs over, the one named last changes fastest.
Arguments:
- hidden_states: bfloat16 [1024, 4, 4096], P('expert'), may hold values from -6 to 6
- routes: int32 [1024, 4, 8], P('expert'), may hold values from 0 to 63, all different within a row; in each aligned block of 64 rows (0 to 63, 64 to 127, ..., all dimensions but the last counted through in order) at most 16 rows name the same one
- route_weight: float32 [1024, 4, 8], P('expert'), may hold values from 0.05 to 1
- finish_step: int32 [1024], P('expert'), may hold values from 1 to 4
- group_keep: int32 [64], P('expert'), may hold values from 0 to 1
- dest_slot: int32 [1024], P('expert'), may hold values from 0 to 1023, as said below
- w_gate: bfloat16 [64, 4096, 1536], P('expert', None, 'dp'), may hold values from -0.09375 to 0.09375
- w_up: bfloat16 [64, 4096, 1536], P('expert', None, 'dp'), may hold values from -0.09375 to 0.09375
- w_down: bfloat16 [64, 1536, 4096], P('expert', 'dp'), may hold values from -0.15625 to 0.15625
Outputs:
- trainer_rows: bfloat16 [1024, 4, 4096], P(('dp', 'expert'))
Inputs may be any that keep to these rules, and one draw needn't show every extreme that they name: `routes`: in the 64 row-steps of one prompt group (rows g * 16 to (g + 1) * 16 - 1, all steps), no expert is named more than 16 times, a bound that some block reaches; a row names 8 different experts at each step. dest_slot is a permutation of the slots; row r of group g = r // 16 goes to a slot (d * 64 + g) * 4 + i with 0 <= d < 4 and 0 <= i < 4.
All inputs are finite; a program needn't handle non-finite values.
Results may differ from a plain program's by a relative error of at most 0.0049.
Values may be sent and summed in bfloat16 or wider, within the bound.
No kernel may reach another device: no remote copies, remote signals or barrier semaphores. Data moves between devices by JAX's collectives and lax.ppermute only.
A program may use at most 128 MiB of HBM per device.

v0:
```python
import jax
import jax.numpy as jnp
from jax import lax
from jax.sharding import PartitionSpec as P

MOST_BASE = 16


def exchange_gather(matrix, replica, replica_count):
    width = matrix.shape[1] // replica_count
    pieces = [lax.dynamic_slice_in_dim(matrix, replica * width, width, axis=1)]
    for shift in range(1, replica_count):
        start = (replica + shift) % replica_count * width
        outgoing = lax.dynamic_slice_in_dim(matrix, start, width, axis=1)
        pairs = [(i, (i + shift) % replica_count) for i in range(replica_count)]
        pieces.append(lax.ppermute(outgoing, "dp", pairs))
    return pieces


def exchange_all(block, replica_count):
    pieces = [block]
    for shift in range(1, replica_count):
        pairs = [(i, (i + shift) % replica_count) for i in range(replica_count)]
        pieces.append(lax.ppermute(block, "dp", pairs))
    return jnp.stack(pieces, axis=0)


def body(
    hidden_states, routes, route_weight, finish_step, group_keep, dest_slot, w_gate, w_up, w_down
):
    expert_count = lax.axis_size("expert")
    replica_count = lax.axis_size("dp")
    replica = lax.axis_index("dp")
    row_count, step_count, model_width = hidden_states.shape
    top_count = routes.shape[2]
    hidden_part = w_down.shape[1]
    columns = model_width // replica_count
    tokens = row_count * step_count
    slot_count = min(tokens, max(MOST_BASE, 2 * tokens * top_count // expert_count))
    slot_count = -(-slot_count // replica_count) * replica_count
    part = slot_count // replica_count
    down_cols = exchange_gather(w_down[0], replica, replica_count)
    step_ids = lax.broadcasted_iota(jnp.int32, (row_count, step_count), 1)
    live_mask = ((step_ids < finish_step[:, None]) & (group_keep[0] == 1)).reshape(tokens)
    gate_share = route_weight / jnp.sum(route_weight, axis=2, keepdims=True)
    expert_ids = lax.broadcasted_iota(jnp.int32, (1, 1, expert_count), 2)
    picked = (routes.reshape(tokens, top_count, 1) == expert_ids) & live_mask[:, None, None]
    hit_mask = jnp.sum(picked.astype(jnp.int32), axis=1)
    share_wide = jnp.broadcast_to(gate_share.reshape(tokens, top_count, 1), picked.shape)
    weight = jnp.sum(jnp.where(picked, share_wide, jnp.zeros_like(share_wide)), axis=1)
    prior_hits = jnp.cumsum(hit_mask, axis=0) - hit_mask
    flat_inputs = hidden_states.reshape(tokens, model_width)
    chunks = 2 if part % 2 == 0 else 1
    sub = part // chunks
    member_ids = lax.broadcasted_iota(jnp.int32, (1, 1, replica_count, 1), 2)
    within_ids = lax.broadcasted_iota(jnp.int32, (1, 1, 1, sub), 3)
    combined = jnp.zeros((tokens, columns), jnp.float32)
    outgoings = []
    for chunk in range(chunks):
        slot_ids = replica * part + chunk * sub + lax.broadcasted_iota(jnp.int32, (1, 1, sub), 2)
        placement = (hit_mask[:, :, None] == 1) & (prior_hits[:, :, None] == slot_ids)
        placement = placement.reshape(tokens, expert_count * sub)
        outgoings.append(
            lax.dot_general(
                placement.astype(jnp.bfloat16),
                flat_inputs,
                (((0,), (0,)), ((), ())),
                preferred_element_type=jnp.float32,
            ).astype(jnp.bfloat16)
        )
    if chunks > 1:
        down_cols, outgoings[1] = lax.optimization_barrier((down_cols, outgoings[1]))
    down_stack = jnp.stack(down_cols, axis=0)
    for chunk in range(chunks):
        outgoing = outgoings[chunk]
        arrived = lax.all_to_all(outgoing, "expert", split_axis=0, concat_axis=0, tiled=True)
        gathered = lax.all_gather(arrived, "dp", axis=0, tiled=True)
        gate_part = jnp.dot(gathered, w_gate[0], preferred_element_type=jnp.float32)
        up_part = jnp.dot(gathered, w_up[0], preferred_element_type=jnp.float32)
        activated = (jax.nn.silu(gate_part) * up_part).astype(jnp.bfloat16)
        hidden_all = exchange_all(activated, replica_count)
        expert_cols = lax.dot_general(
            hidden_all, down_stack, (((0, 2), (0, 1)), ((), ())), preferred_element_type=jnp.float32
        ).astype(jnp.bfloat16)
        by_source = expert_cols.reshape(replica_count, expert_count, sub, columns).transpose(
            1, 0, 2, 3
        )
        returned_rows = lax.all_to_all(by_source, "expert", split_axis=0, concat_axis=0, tiled=True)
        all_slot_ids = member_ids * part + chunk * sub + within_ids
        weighted_place = jnp.where(
            (hit_mask[:, :, None, None] == 1) & (prior_hits[:, :, None, None] == all_slot_ids),
            weight[:, :, None, None],
            0.0,
        ).reshape(tokens, expert_count * replica_count * sub)
        combined = combined + jnp.dot(
            weighted_place,
            returned_rows.reshape(expert_count * replica_count * sub, columns).astype(jnp.float32),
            precision=lax.Precision.HIGH,
            preferred_element_type=jnp.float32,
        )
    share_rows = row_count // replica_count
    flat_device = dest_slot // share_rows
    target = flat_device // expert_count * share_rows + dest_slot % share_rows
    position_ids = lax.broadcasted_iota(jnp.int32, (replica_count * share_rows, row_count), 0)
    arrangement = (target[None, :] == position_ids).astype(jnp.bfloat16)
    arranged = jnp.dot(
        arrangement,
        combined.astype(jnp.bfloat16).reshape(row_count, step_count * columns),
        preferred_element_type=jnp.float32,
    ).astype(jnp.bfloat16)
    arranged = arranged.reshape(replica_count, share_rows, step_count, columns)
    quarters = lax.all_to_all(arranged, "dp", split_axis=0, concat_axis=0, tiled=True)
    return quarters.transpose(1, 2, 0, 3).reshape(share_rows, step_count, model_width)


def solution(mesh):
    in_specs = (
        P("expert", None, None),
        P("expert", None, None),
        P("expert", None, None),
        P("expert"),
        P("expert"),
        P("expert"),
        P("expert", None, "dp"),
        P("expert", None, "dp"),
        P("expert", "dp", None),
    )
    out_specs = P(("dp", "expert"), None, None)
    return jax.shard_map(body, mesh=mesh, in_specs=in_specs, out_specs=out_specs, check_vma=False)
```

profile of v0, /device:TPU:2, one launch (start us, length us, event | category | flops | bytes accessed | tf_op | source)
XLA Modules:
  0.0 302.3 jit_solution(9261390843322471953)
XLA Ops:
  6.5 3.7 %dynamic-slice_bitcast_fusion = (bf16[384,1024]{1,0:T(8,128)(2,1)}, bf16[384,1024]{1,0:T(8,128)(2,1)}, bf16[384,1024]{1,0:T(8,128)(2,1)}, bf16[384,1024]{1,0:T(8,128)(2,1)}) fusion(bf16[1,384,4096]{2,1,0:T(8,128)(2,1)} %param.17, s32[]{:T(128)S(6)} %select_n.63, s32[]{:T(128)S(6)} %select_n.59, s32[]{:T(128)S(6)} %select_n.57, s32[]{:T(128)S(6)} %select_n.61), kind=kLoop, calls=%fused_computation.40 | loop fusion | bytes 6291472 | tf_op jit(solution)/shard_map/dynamic_slice | solution.py:14
  10.3 1.6 collective-permute-start.3
  11.9 2.9 collective-permute-start.4
  14.8 1.3 collective-permute-start.5
  17.0 0.2 convert_reduce_fusion
  17.8 2.0 reshape.213
  19.7 2.4 convolution_convert_fusion
  22.2 9.0 %collective-permute-done.3 = bf16[384,1024]{1,0:T(8,128)(2,1)} collective-permute-done((bf16[384,1024]{1,0:T(8,128)(2,1)}, bf16[384,1024]{1,0:T(8,128)(2,1)}, u32[]{:S(2)}, u32[]{:S(2)}) %collective-permute-start.3) | collective-permute-done | bytes 786464 | tf_op jit(solution)/shard_map/ppermute | solution.py:16
  31.2 18.0 %collective-permute-done.4 = bf16[384,1024]{1,0:T(8,128)(2,1)} collective-permute-done((bf16[384,1024]{1,0:T(8,128)(2,1)}, bf16[384,1024]{1,0:T(8,128)(2,1)}, u32[]{:S(2)}, u32[]{:S(2)}) %collective-permute-start.4) | collective-permute-done | bytes 786464 | tf_op jit(solution)/shard_map/ppermute | solution.py:16
  49.2 2.5 all_to_all.29
  51.7 40.9 %all_to_all.39 = bf16[64,2,4096]{2,1,0:T(2,128)(2,1)} all-to-all(bf16[64,2,4096]{2,1,0:T(2,128)(2,1)} %all_to_all.29), channel_id=1, replica_groups=mesh['dp'=4,'expert'=64] {'expert'}, dimensions={0} | all-to-all | bytes 2097152 | tf_op jit(solution)/shard_map/all_to_all | solution.py:76
  92.7 2.3 all_to_all.31
  95.1 2.4 convolution_convert_fusion.1
  97.5 2.5 all_to_all.25
  100.1 34.6 %all_to_all.40 = bf16[64,2,4096]{2,1,0:T(2,128)(2,1)} all-to-all(bf16[64,2,4096]{2,1,0:T(2,128)(2,1)} %all_to_all.25), channel_id=1, replica_groups=mesh['dp'=4,'expert'=64] {'expert'}, dimensions={0} | all-to-all | bytes 2097152 | tf_op jit(solution)/shard_map/all_to_all | solution.py:76
  134.6 2.3 all_to_all.27
  136.9 5.0 %all-gather.5.cloned.1.call-done = bf16[512,4096]{1,0:T(8,128)(2,1)} async-done(((bf16[128,4096]{1,0:T(8,128)(2,1)}), bf16[512,4096]{1,0:T(8,128)(2,1)}) %all-gather.5.cloned.1.call-update) | async-done | bytes 4194320 | tf_op jit(solution)/shard_map/all_gather | solution.py:77
  142.0 4.7 %fusion.4 = f32[512,384]{1,0:T(8,128)S(1)} fusion(bf16[512,4096]{1,0:T(8,128)(2,1)} %all-gather.5.cloned.1.call-done, bf16[1,4096,384]{2,1,0:T(8,128)(2,1)S(1)} %copy-done), kind=kOutput, calls=%fused_computation.8 | convolution fusion | flops 1610612736 | bytes 8126464 | tf_op jit(solution)/shard_map/dot_general | solution.py:78
  146.7 2.3 fusion.28
  149.0 1.2 collective-permute-start.8
  150.2 1.8 collective-permute-start.7
  152.0 0.6 collective-permute-start.6
  152.6 9.2 %collective-permute-done.8 = bf16[512,384]{1,0:T(8,128)(2,1)S(1)} collective-permute-done((bf16[512,384]{1,0:T(8,128)(2,1)S(1)}, bf16[512,384]{1,0:T(8,128)(2,1)S(1)}, u32[]{:S(2)}, u32[]{:S(2)}) %collective-permute-start.8) | collective-permute-done | bytes 393248 | tf_op jit(solution)/shard_map/ppermute | solution.py:24
  161.8 4.5 %collective-permute-done.7 = bf16[512,384]{1,0:T(8,128)(2,1)S(1)} collective-permute-done((bf16[512,384]{1,0:T(8,128)(2,1)S(1)}, bf16[512,384]{1,0:T(8,128)(2,1)S(1)}, u32[]{:S(2)}, u32[]{:S(2)}) %collective-permute-start.7) | collective-permute-done | bytes 393248 | tf_op jit(solution)/shard_map/ppermute | solution.py:24
  166.3 14.4 %collective-permute-done.6 = bf16[512,384]{1,0:T(8,128)(2,1)S(1)} collective-permute-done((bf16[512,384]{1,0:T(8,128)(2,1)S(1)}, bf16[512,384]{1,0:T(8,128)(2,1)S(1)}, u32[]{:S(2)}, u32[]{:S(2)}) %collective-permute-start.6) | collective-permute-done | bytes 393248 | tf_op jit(solution)/shard_map/ppermute | solution.py:24
  180.7 4.5 %bitcast_convert_fusion = bf16[512,1024]{1,0:T(8,128)(2,1)} fusion(bf16[1,512,384]{2,1,0:T(8,128)(2,1)S(1)} %bitcast.91, bf16[1,512,384]{2,1,0:T(8,128)(2,1)S(1)} %bitcast.93, bf16[1,512,384]{2,1,0:T(8,128)(2,1)S(1)} %bitcast.94, bf16[1,512,384]{2,1,0:T(8,128)(2,1)S(1)} %bitcast.88, bf16[1,384,1024]{2,1,0:T(8,128)(2,1)} %bitcast.16, ...), kind=kOutput, calls=%fused_computation.12 | convolution fusion | flops 1618214912 | bytes 5767168 | tf_op jit(solution)/shard_map/dot_general | solution.py:82
  185.2 2.2 reshape.215
  187.5 3.4 %copy.47 = bf16[4,64,2,1024]{3,2,0,1:T(2,128)(2,1)} copy(bf16[4,64,2,1024]{3,2,1,0:T(2,128)(2,1)} %reshape.215) | data formatting | bytes 2097152 | tf_op jit(solution)/shard_map/reshape | solution.py:85
  190.8 10.7 %all-to-all-start.3 = ((bf16[64,4,2,1024]{3,2,1,0:T(2,128)(2,1)}), bf16[64,4,2,1024]{3,2,1,0:T(2,128)(2,1)}, u32[]{:S(2)}, u32[]{:S(2)}) async-start(bf16[64,4,2,1024]{3,2,1,0:T(2,128)(2,1)} %bitcast.79), calls=%async_computation.3 | async-start | bytes 2097152 | tf_op jit(solution)/shard_map/all_to_all | solution.py:88
  201.6 3.2 %all-gather.3.cloned.1.call-done = bf16[512,4096]{1,0:T(8,128)(2,1)} async-done(((bf16[128,4096]{1,0:T(8,128)(2,1)}), bf16[512,4096]{1,0:T(8,128)(2,1)}) %all-gather.3.cloned.1.call-update) | async-done | bytes 4194320 | tf_op jit(solution)/shard_map/all_gather | solution.py:77
  204.8 4.7 %fusion.6 = f32[512,384]{1,0:T(8,128)S(1)} fusion(bf16[512,4096]{1,0:T(8,128)(2,1)} %all-gather.3.cloned.1.call-done, bf16[1,4096,384]{2,1,0:T(8,128)(2,1)S(1)} %copy-done), kind=kOutput, calls=%fused_computation.10 | convolution fusion | flops 1610612736 | bytes 8126464 | tf_op jit(solution)/shard_map/dot_general | solution.py:78
  209.5 2.3 fusion.31
  211.8 0.7 collective-permute-start.2
  212.5 1.8 collective-permute-start.1
  214.3 0.8 collective-permute-start
  215.1 8.8 %collective-permute-done.2 = bf16[512,384]{1,0:T(8,128)(2,1)S(1)} collective-permute-done((bf16[512,384]{1,0:T(8,128)(2,1)S(1)}, bf16[512,384]{1,0:T(8,128)(2,1)S(1)}, u32[]{:S(2)}, u32[]{:S(2)}) %collective-permute-start.2) | collective-permute-done | bytes 393248 | tf_op jit(solution)/shard_map/ppermute | solution.py:24
  223.9 2.2 collective-permute-done.1
  226.1 7.2 %collective-permute-done = bf16[512,384]{1,0:T(8,128)(2,1)S(1)} collective-permute-done((bf16[512,384]{1,0:T(8,128)(2,1)S(1)}, bf16[512,384]{1,0:T(8,128)(2,1)S(1)}, u32[]{:S(2)}, u32[]{:S(2)}) %collective-permute-start) | collective-permute-done | bytes 393248 | tf_op jit(solution)/shard_map/ppermute | solution.py:24
  233.3 4.4 %bitcast_convert_fusion.1 = bf16[512,1024]{1,0:T(8,128)(2,1)} fusion(bf16[1,512,384]{2,1,0:T(8,128)(2,1)S(1)} %bitcast.89, bf16[1,512,384]{2,1,0:T(8,128)(2,1)S(1)} %bitcast.90, bf16[1,512,384]{2,1,0:T(8,128)(2,1)S(1)} %bitcast.92, bf16[1,512,384]{2,1,0:T(8,128)(2,1)S(1)} %bitcast.87, bf16[1,384,1024]{2,1,0:T(8,128)(2,1)} %bitcast.16, ...), kind=kOutput, calls=%fused_computation.13 | convolution fusion | flops 1618214912 | bytes 5767168 | tf_op jit(solution)/shard_map/dot_general | solution.py:82
  237.7 2.3 reshape.214
  239.9 3.4 %copy.48 = bf16[4,64,2,1024]{3,2,0,1:T(2,128)(2,1)} copy(bf16[4,64,2,1024]{3,2,1,0:T(2,128)(2,1)} %reshape.214) | data formatting | bytes 2097152 | tf_op jit(solution)/shard_map/reshape | solution.py:85
  243.3 10.7 %all-to-all-start.1 = ((bf16[64,4,2,1024]{3,2,1,0:T(2,128)(2,1)}), bf16[64,4,2,1024]{3,2,1,0:T(2,128)(2,1)}, u32[]{:S(2)}, u32[]{:S(2)}) async-start(bf16[64,4,2,1024]{3,2,1,0:T(2,128)(2,1)} %bitcast.80), calls=%async_computation.1 | async-start | bytes 2097152 | tf_op jit(solution)/shard_map/all_to_all | solution.py:88
  254.2 0.3 select_reduce_fusion
  254.7 3.5 %convolution_bitcast_fusion = f32[64,1024]{1,0:T(8,128)} fusion(bf16[64,4,2,1024]{3,2,1,0:T(2,128)(2,1)} %all-to-all-done.3, s32[4,2]{1,0:T(4,128)S(1)} %iota_add_fusion, f32[64,64]{1,0:T(8,128)S(1)} %select_reduce_fusion, s32[64,64]{1,0:T(8,128)S(1)} %sub.20, pred[64,64]{1,0:T(8,128)(4,1)S(1)} %broadcast_compare_fusion), kind=kOutput, calls=%fused_computation.32 | convolution fusion | flops 201424896 | bytes 1347616 | tf_op jit(solution)/shard_map/dot_general | solution.py:95
  258.2 24.6 %all-to-all-done.1 = bf16[64,4,2,1024]{3,2,1,0:T(2,128)(2,1)} async-done(((bf16[64,4,2,1024]{3,2,1,0:T(2,128)(2,1)}), bf16[64,4,2,1024]{3,2,1,0:T(2,128)(2,1)}, u32[]{:S(2)}, u32[]{:S(2)}) %all-to-all-start.1) | async-done | bytes 1048608 | tf_op jit(solution)/shard_map/all_to_all | solution.py:88
  282.8 2.8 fusion.35
  285.9 8.8 %all_to_all.41 = bf16[4,4,4,1024]{3,2,1,0:T(4,128)(2,1)S(1)} all-to-all(bf16[4,4,4,1024]{3,2,1,0:T(4,128)(2,1)S(1)} %reshape.217), channel_id=1, replica_groups=mesh['dp'=4,'expert'=64] {'dp'}, dimensions={0} | all-to-all | bytes 262144 | tf_op jit(solution)/shard_map/all_to_all | solution.py:112
  294.7 0.7 copy.40
  (51 shorter events, 1.5 us)
Async XLA Ops:
  6.5 135.4 %copy-start = (bf16[1,4096,384]{2,1,0:T(8,128)(2,1)S(1)}, bf16[1,4096,384]{2,1,0:T(8,128)(2,1)}, u32[]{:S(2)}) copy-start(bf16[1,4096,384]{2,1,0:T(8,128)(2,1)} %param.15) | copy-start | bytes 9437188
  6.5 135.4 %all-gather.5.cloned.1.call-start = ((), (), s32[]{:S(2)}) async-start(), calls=%async_computation.6 | async-start | bytes 5242880 | tf_op jit(solution)/shard_map/all_gather | solution.py:77
  6.5 9.6 %copy-start.4 = (s32[16,4,8]{0,2,1:T(8,128)S(1)}, s32[16,4,8]{0,2,1:T(8,128)}, u32[]{:S(2)}) copy-start(s32[16,4,8]{0,2,1:T(8,128)} %param.10) | copy-start | bytes 6148
  6.5 10.3 %copy-start.5 = (s32[16]{0:T(128)S(1)}, s32[16]{0:T(128)}, u32[]{:S(2)}) copy-start(s32[16]{0:T(128)} %param.12) | copy-start | bytes 196
  10.3 20.9 %collective-permute-start.3 = (bf16[384,1024]{1,0:T(8,128)(2,1)}, bf16[384,1024]{1,0:T(8,128)(2,1)}, u32[]{:S(2)}, u32[]{:S(2)}) collective-permute-start(bf16[384,1024]{1,0:T(8,128)(2,1)} %get-tuple-element.16), channel_id=1, source_target_pairs={{0,64},{64,128},{128,192},{192,0},{1,65},{65,129},{129,193},{193,1... | collective-permute-start | bytes 2359304 | tf_op jit(solution)/shard_map/ppermute | solution.py:16
  11.9 37.3 %collective-permute-start.4 = (bf16[384,1024]{1,0:T(8,128)(2,1)}, bf16[384,1024]{1,0:T(8,128)(2,1)}, u32[]{:S(2)}, u32[]{:S(2)}) collective-permute-start(bf16[384,1024]{1,0:T(8,128)(2,1)} %get-tuple-element.18), channel_id=1, source_target_pairs={{0,128},{64,192},{128,0},{192,64},{1,129},{65,193},{129,1},{193,65... | collective-permute-start | bytes 2359304 | tf_op jit(solution)/shard_map/ppermute | solution.py:16
  14.8 34.4 %collective-permute-start.5 = (bf16[384,1024]{1,0:T(8,128)(2,1)}, bf16[384,1024]{1,0:T(8,128)(2,1)}, u32[]{:S(2)}, u32[]{:S(2)}) collective-permute-start(bf16[384,1024]{1,0:T(8,128)(2,1)} %get-tuple-element.15), channel_id=1, source_target_pairs={{0,192},{64,0},{128,64},{192,128},{1,193},{65,1},{129,65},{193,129... | collective-permute-start | bytes 2359304 | tf_op jit(solution)/shard_map/ppermute | solution.py:16
  95.0 109.8 %all-gather.3.cloned.1.call-start = ((), (), s32[]{:S(2)}) async-start(), calls=%async_computation.5 | async-start | bytes 5242880 | tf_op jit(solution)/shard_map/all_gather | solution.py:77
  142.0 4.7 %copy-start.7 = (bf16[512,4096]{1,0:T(8,128)(2,1)S(1)}, bf16[512,4096]{1,0:T(8,128)(2,1)}, u32[]{:S(2)}) copy-start(bf16[512,4096]{1,0:T(8,128)(2,1)} %all-gather.5.cloned.1.call-done) | copy-start | bytes 12582916
  142.0 4.7 %copy-start.8 = (bf16[1,4096,384]{2,1,0:T(8,128)(2,1)S(1)}, bf16[1,4096,384]{2,1,0:T(8,128)(2,1)}, u32[]{:S(2)}) copy-start(bf16[1,4096,384]{2,1,0:T(8,128)(2,1)} %param.16) | copy-start | bytes 9437188
  146.6 34.1 %copy-start.1 = (bf16[384,1024]{1,0:T(8,128)(2,1)S(1)}, bf16[384,1024]{1,0:T(8,128)(2,1)}, u32[]{:S(2)}) copy-start(bf16[384,1024]{1,0:T(8,128)(2,1)} %get-tuple-element.10) | copy-start | bytes 2359300
  149.0 12.8 %collective-permute-start.8 = (bf16[512,384]{1,0:T(8,128)(2,1)S(1)}, bf16[512,384]{1,0:T(8,128)(2,1)S(1)}, u32[]{:S(2)}, u32[]{:S(2)}) collective-permute-start(bf16[512,384]{1,0:T(8,128)(2,1)S(1)} %fusion.28), channel_id=1, source_target_pairs={{0,192},{64,0},{128,64},{192,128},{1,193},{65,1},{129,65},{193,129... | collective-permute-start | bytes 1179656 | tf_op jit(solution)/shard_map/ppermute | solution.py:24
  150.2 16.1 %collective-permute-start.7 = (bf16[512,384]{1,0:T(8,128)(2,1)S(1)}, bf16[512,384]{1,0:T(8,128)(2,1)S(1)}, u32[]{:S(2)}, u32[]{:S(2)}) collective-permute-start(bf16[512,384]{1,0:T(8,128)(2,1)S(1)} %fusion.28), channel_id=1, source_target_pairs={{0,128},{64,192},{128,0},{192,64},{1,129},{65,193},{129,1},{193,65... | collective-permute-start | bytes 1179656 | tf_op jit(solution)/shard_map/ppermute | solution.py:24
  152.0 28.7 %collective-permute-start.6 = (bf16[512,384]{1,0:T(8,128)(2,1)S(1)}, bf16[512,384]{1,0:T(8,128)(2,1)S(1)}, u32[]{:S(2)}, u32[]{:S(2)}) collective-permute-start(bf16[512,384]{1,0:T(8,128)(2,1)S(1)} %fusion.28), channel_id=1, source_target_pairs={{0,64},{64,128},{128,192},{192,0},{1,65},{65,129},{129,193},{193,1... | collective-permute-start | bytes 1179656 | tf_op jit(solution)/shard_map/ppermute | solution.py:24
  190.8 52.5 %all-to-all-start.3 = ((bf16[64,4,2,1024]{3,2,1,0:T(2,128)(2,1)}), bf16[64,4,2,1024]{3,2,1,0:T(2,128)(2,1)}, u32[]{:S(2)}, u32[]{:S(2)}) async-start(bf16[64,4,2,1024]{3,2,1,0:T(2,128)(2,1)} %bitcast.79), calls=%async_computation.3 | async-start | bytes 2097152 | tf_op jit(solution)/shard_map/all_to_all | solution.py:88
  204.8 4.7 %copy-start.6 = (bf16[512,4096]{1,0:T(8,128)(2,1)S(1)}, bf16[512,4096]{1,0:T(8,128)(2,1)}, u32[]{:S(2)}) copy-start(bf16[512,4096]{1,0:T(8,128)(2,1)} %all-gather.3.cloned.1.call-done) | copy-start | bytes 12582916
  204.8 4.7 %copy-start.9 = (bf16[1,4096,384]{2,1,0:T(8,128)(2,1)S(1)}, bf16[1,4096,384]{2,1,0:T(8,128)(2,1)}, u32[]{:S(2)}) copy-start(bf16[1,4096,384]{2,1,0:T(8,128)(2,1)} %param.16) | copy-start | bytes 9437188
  209.5 23.8 %copy-start.2 = (bf16[384,1024]{1,0:T(8,128)(2,1)S(1)}, bf16[384,1024]{1,0:T(8,128)(2,1)}, u32[]{:S(2)}) copy-start(bf16[384,1024]{1,0:T(8,128)(2,1)} %get-tuple-element.10) | copy-start | bytes 2359300
  211.8 12.0 %collective-permute-start.2 = (bf16[512,384]{1,0:T(8,128)(2,1)S(1)}, bf16[512,384]{1,0:T(8,128)(2,1)S(1)}, u32[]{:S(2)}, u32[]{:S(2)}) collective-permute-start(bf16[512,384]{1,0:T(8,128)(2,1)S(1)} %fusion.31), channel_id=1, source_target_pairs={{0,192},{64,0},{128,64},{192,128},{1,193},{65,1},{129,65},{193,129... | collective-permute-start | bytes 1179656 | tf_op jit(solution)/shard_map/ppermute | solution.py:24
  212.5 13.6 %collective-permute-start.1 = (bf16[512,384]{1,0:T(8,128)(2,1)S(1)}, bf16[512,384]{1,0:T(8,128)(2,1)S(1)}, u32[]{:S(2)}, u32[]{:S(2)}) collective-permute-start(bf16[512,384]{1,0:T(8,128)(2,1)S(1)} %fusion.31), channel_id=1, source_target_pairs={{0,128},{64,192},{128,0},{192,64},{1,129},{65,193},{129,1},{193,65... | collective-permute-start | bytes 1179656 | tf_op jit(solution)/shard_map/ppermute | solution.py:24
  214.3 18.9 %collective-permute-start = (bf16[512,384]{1,0:T(8,128)(2,1)S(1)}, bf16[512,384]{1,0:T(8,128)(2,1)S(1)}, u32[]{:S(2)}, u32[]{:S(2)}) collective-permute-start(bf16[512,384]{1,0:T(8,128)(2,1)S(1)} %fusion.31), channel_id=1, source_target_pairs={{0,64},{64,128},{128,192},{192,0},{1,65},{65,129},{129,193},{193,1... | collective-permute-start | bytes 1179656 | tf_op jit(solution)/shard_map/ppermute | solution.py:24
  237.7 16.4 %copy-start.3 = (f32[16,4,8]{0,2,1:T(8,128)S(1)}, f32[16,4,8]{0,2,1:T(8,128)}, u32[]{:S(2)}) copy-start(f32[16,4,8]{0,2,1:T(8,128)} %param.11) | copy-start | bytes 6148
  237.7 16.8 %copy-start.10 = (s32[16]{0:T(128)S(1)}, s32[16]{0:T(128)}, u32[]{:S(2)}) copy-start(s32[16]{0:T(128)} %param.14) | copy-start | bytes 196
  243.3 39.5 %all-to-all-start.1 = ((bf16[64,4,2,1024]{3,2,1,0:T(2,128)(2,1)}), bf16[64,4,2,1024]{3,2,1,0:T(2,128)(2,1)}, u32[]{:S(2)}, u32[]{:S(2)}) async-start(bf16[64,4,2,1024]{3,2,1,0:T(2,128)(2,1)} %bitcast.80), calls=%async_computation.1 | async-start | bytes 2097152 | tf_op jit(solution)/shard_map/all_to_all | solution.py:88
Sparse Core Ops, SparseCore 0:
  95.1 46.8 all-gather.4
  143.8 60.9 all-gather.2
where the time goes:
time: 303 us; the launch traced here: 302 us
  waiting for transfers between devices  106 us (35%)
  blocking collectives  84.3 us (28%)
  matrix products  34.3 us (11%)
  starting transfers between devices  34.2 us (11%)
  local copies, waits for them, and re-layouts  28 us (9%)
  between operations  14.3 us (5%)
    all_to_all x2, blocking collectives, body(): lax.all_to_all(outgoing, 'expert', split_axis=0, concat_axis=0, tiled=True)  75.5 us
    ppermute x6, waiting for transfers between devices, exchange_all(): pieces.append(lax.ppermute(block, 'dp', pairs))  46.3 us
    ppermute x3, waiting for transfers between devices, exchange_gather(): pieces.append(lax.ppermute(outgoing, 'dp', pairs))  27 us
    all_to_all x2, waiting for transfers between devices, body(): lax.all_to_all(by_source, 'expert', split_axis=0, concat_axis=0, tiled=True)  24.6 us
    all_to_all x2, starting transfers between devices, body(): lax.all_to_all(by_source, 'expert', split_axis=0, concat_axis=0, tiled=True)  21.5 us
    reshape x4, local copies, waits for them, and re-layouts, body(): expert_cols.reshape(replica_count, expert_count, sub, columns)  11.2 us
    all_to_all x4, local copies, waits for them, and re-layouts, body(): lax.all_to_all(outgoing, 'expert', split_axis=0, concat_axis=0, tiled=True)  9.66 us
    dot_general x2, matrix products, body(): gate_part = jnp.dot(gathered, w_gate[0], preferred_element_type=jnp.float32)  9.32 us
  transfers between devices with their start and end apart: 13, of which 11 were waited for; matrix products, arithmetic and copies ran while one was open for 15% of the time, Pallas kernels for 0%

commit v1 on v0

--- a/solution.py
+++ b/solution.py
@@ -4,6 +4,17 @@
 from jax.sharding import PartitionSpec as P
 
 MOST_BASE = 16
+
+
+def test_figure_here(row_data, along_dim, values):
+    front, piece_now = (row_data.shape[:along_dim], row_data.shape[along_dim + 1 :])
+    return jnp.moveaxis(row_data.reshape(*front, values, -1, *piece_now), along_dim, 0)
+
+
+def digits_proceed(arr, at_axis):
+    arr = jnp.moveaxis(arr, 0, at_axis)
+    y = arr.shape
+    return arr.reshape(*y[:at_axis], y[at_axis] * y[at_axis + 1], *y[at_axis + 2 :])
 
 
 def exchange_gather(matrix, replica, replica_count):
@@ -109,7 +120,18 @@
         preferred_element_type=jnp.float32,
     ).astype(jnp.bfloat16)
     arranged = arranged.reshape(replica_count, share_rows, step_count, columns)
-    quarters = lax.all_to_all(arranged, "dp", split_axis=0, concat_axis=0, tiled=True)
+    block_next = lax.axis_size("dp")
+    g_now = lax.axis_index("dp")
+    f_next, frame_out = (block_next, g_now)
+    reached = test_figure_here(arranged, 0, f_next)
+    kk = 1
+    leaves = [reached[frame_out]]
+    while kk < f_next:
+        all_rows = reached[frame_out ^ kk]
+        leaves.append(lax.ppermute(all_rows, "dp", [(m, m ^ kk) for m in range(f_next)]))
+        kk += 1
+    reached = jnp.stack(leaves, axis=0)[frame_out ^ jnp.arange(f_next)]
+    quarters = digits_proceed(reached, 0)
     return quarters.transpose(1, 2, 0, 3).reshape(share_rows, step_count, model_width)
 
 

time: 303 us -> 302 us (level)
  blocking collectives: 84.3 us -> 75.5 us
  starting transfers between devices: 34.2 us -> 38.3 us
    all_to_all x1 -> x0, blocking collectives: 8.79 us -> none  [body(): lax.all_to_all(arranged, 'dp', split_axis=0, concat_axis=0, tiled=True)]
    ppermute x0 -> x3, starting transfers between devices: none -> 4.18 us  [body(): lax.ppermute(all_rows, 'dp', [(m, m ^ kk) for m in range(f_next)])]
  transfers between devices with their start and end apart: 13 -> 16, of which waited for: 11 -> 14; matrix products, arithmetic and copies ran while one was open for 15% -> 15% of each run, Pallas kernels for 0% -> 0%
where the time goes in v1:
time: 302 us; the launch traced here: 301 us
  waiting for transfers between devices  108 us (36%)
  blocking collectives  75.5 us (25%)
  starting transfers between devices  38.3 us (13%)
  matrix products  34.4 us (11%)
  local copies, waits for them, and re-layouts  28.7 us (10%)
  between operations  14.3 us (5%)
    all_to_all x2, blocking collectives, body(): lax.all_to_all(outgoing, 'expert', split_axis=0, concat_axis=0, tiled=True)  75.5 us
    ppermute x6, waiting for transfers between devices, exchange_all(): pieces.append(lax.ppermute(block, 'dp', pairs))  46.3 us
    ppermute x3, waiting for transfers between devices, exchange_gather(): pieces.append(lax.ppermute(outgoing, 'dp', pairs))  27 us
    all_to_all x2, waiting for transfers between devices, body(): lax.all_to_all(by_source, 'expert', split_axis=0, concat_axis=0, tiled=True)  24.6 us
    all_to_all x2, starting transfers between devices, body(): lax.all_to_all(by_source, 'expert', split_axis=0, concat_axis=0, tiled=True)  21.5 us
    reshape x4, local copies, waits for them, and re-layouts, body(): expert_cols.reshape(replica_count, expert_count, sub, columns)  11.2 us
    all_to_all x4, local copies, waits for them, and re-layouts, body(): lax.all_to_all(outgoing, 'expert', split_axis=0, concat_axis=0, tiled=True)  9.65 us
    dot_general x2, matrix products, body(): gate_part = jnp.dot(gathered, w_gate[0], preferred_element_type=jnp.float32)  9.32 us
  transfers between devices with their start and end apart: 16, of which 14 were waited for; matrix products, arithmetic and copies ran while one was open for 15% of the time, Pallas kernels for 0%

profile of v1, /device:TPU:2, one launch (start us, length us, event | category | flops | bytes accessed | tf_op | source)
XLA Modules:
  0.0 300.8 jit_solution(7558365815671758302)
XLA Ops:
  6.5 3.7 %dynamic-slice_bitcast_fusion = (bf16[384,1024]{1,0:T(8,128)(2,1)}, bf16[384,1024]{1,0:T(8,128)(2,1)}, bf16[384,1024]{1,0:T(8,128)(2,1)}, bf16[384,1024]{1,0:T(8,128)(2,1)}) fusion(bf16[1,384,4096]{2,1,0:T(8,128)(2,1)} %param.17, s32[]{:T(128)S(6)} %select_n.85, s32[]{:T(128)S(6)} %select_n.81, s32[]{:T(128)S(6)} %select_n.79, s32[]{:T(128)S(6)} %select_n.83), kind=kLoop, calls=%fused_computation.41 | loop fusion | bytes 6291472 | tf_op jit(solution)/shard_map/dynamic_slice | solution.py:25
  10.3 1.6 collective-permute-start.3
  11.9 2.9 collective-permute-start.4
  14.8 1.3 collective-permute-start.5
  17.8 2.0 reshape.229
  19.7 2.5 convolution_convert_fusion
  22.2 8.9 %collective-permute-done.3 = bf16[384,1024]{1,0:T(8,128)(2,1)} collective-permute-done((bf16[384,1024]{1,0:T(8,128)(2,1)}, bf16[384,1024]{1,0:T(8,128)(2,1)}, u32[]{:S(2)}, u32[]{:S(2)}) %collective-permute-start.3) | collective-permute-done | bytes 786464 | tf_op jit(solution)/shard_map/ppermute | solution.py:27
  31.2 18.0 %collective-permute-done.4 = bf16[384,1024]{1,0:T(8,128)(2,1)} collective-permute-done((bf16[384,1024]{1,0:T(8,128)(2,1)}, bf16[384,1024]{1,0:T(8,128)(2,1)}, u32[]{:S(2)}, u32[]{:S(2)}) %collective-permute-start.4) | collective-permute-done | bytes 786464 | tf_op jit(solution)/shard_map/ppermute | solution.py:27
  49.2 2.5 all_to_all.26
  51.7 40.9 %all_to_all.34 = bf16[64,2,4096]{2,1,0:T(2,128)(2,1)} all-to-all(bf16[64,2,4096]{2,1,0:T(2,128)(2,1)} %all_to_all.26), channel_id=1, replica_groups=mesh['dp'=4,'expert'=64] {'expert'}, dimensions={0} | all-to-all | bytes 2097152 | tf_op jit(solution)/shard_map/all_to_all | solution.py:87
  92.6 2.3 all_to_all.28
  95.1 2.5 convolution_convert_fusion.1
  97.5 2.5 all_to_all.22
  100.1 34.5 %all_to_all.35 = bf16[64,2,4096]{2,1,0:T(2,128)(2,1)} all-to-all(bf16[64,2,4096]{2,1,0:T(2,128)(2,1)} %all_to_all.22), channel_id=1, replica_groups=mesh['dp'=4,'expert'=64] {'expert'}, dimensions={0} | all-to-all | bytes 2097152 | tf_op jit(solution)/shard_map/all_to_all | solution.py:87
  134.6 2.3 all_to_all.24
  136.9 5.0 %all-gather.5.cloned.1.call-done = bf16[512,4096]{1,0:T(8,128)(2,1)} async-done(((bf16[128,4096]{1,0:T(8,128)(2,1)}), bf16[512,4096]{1,0:T(8,128)(2,1)}) %all-gather.5.cloned.1.call-update) | async-done | bytes 4194320 | tf_op jit(solution)/shard_map/all_gather | solution.py:88
  142.0 4.7 %fusion.4 = f32[512,384]{1,0:T(8,128)S(1)} fusion(bf16[512,4096]{1,0:T(8,128)(2,1)} %all-gather.5.cloned.1.call-done, bf16[1,4096,384]{2,1,0:T(8,128)(2,1)S(1)} %copy-done), kind=kOutput, calls=%fused_computation.9 | convolution fusion | flops 1610612736 | bytes 8126464 | tf_op jit(solution)/shard_map/dot_general | solution.py:89
  146.6 2.3 fusion.28
  149.0 1.2 collective-permute-start.8
  150.2 1.8 collective-permute-start.7
  152.6 9.2 %collective-permute-done.8 = bf16[512,384]{1,0:T(8,128)(2,1)S(1)} collective-permute-done((bf16[512,384]{1,0:T(8,128)(2,1)S(1)}, bf16[512,384]{1,0:T(8,128)(2,1)S(1)}, u32[]{:S(2)}, u32[]{:S(2)}) %collective-permute-start.8) | collective-permute-done | bytes 393248 | tf_op jit(solution)/shard_map/ppermute | solution.py:35
  161.8 4.5 %collective-permute-done.7 = bf16[512,384]{1,0:T(8,128)(2,1)S(1)} collective-permute-done((bf16[512,384]{1,0:T(8,128)(2,1)S(1)}, bf16[512,384]{1,0:T(8,128)(2,1)S(1)}, u32[]{:S(2)}, u32[]{:S(2)}) %collective-permute-start.7) | collective-permute-done | bytes 393248 | tf_op jit(solution)/shard_map/ppermute | solution.py:35
  166.2 14.4 %collective-permute-done.6 = bf16[512,384]{1,0:T(8,128)(2,1)S(1)} collective-permute-done((bf16[512,384]{1,0:T(8,128)(2,1)S(1)}, bf16[512,384]{1,0:T(8,128)(2,1)S(1)}, u32[]{:S(2)}, u32[]{:S(2)}) %collective-permute-start.6) | collective-permute-done | bytes 393248 | tf_op jit(solution)/shard_map/ppermute | solution.py:35
  180.7 4.5 %bitcast_convert_fusion = bf16[512,1024]{1,0:T(8,128)(2,1)} fusion(bf16[1,512,384]{2,1,0:T(8,128)(2,1)S(1)} %bitcast.107, bf16[1,512,384]{2,1,0:T(8,128)(2,1)S(1)} %bitcast.109, bf16[1,512,384]{2,1,0:T(8,128)(2,1)S(1)} %bitcast.110, bf16[1,512,384]{2,1,0:T(8,128)(2,1)S(1)} %bitcast.104, bf16[1,384,1024]{2,1,0:T(8,128)(2,1)} %bitcast.16, ...), kind=kOutput, calls=%fused_computation.13 | convolution fusion | flops 1618214912 | bytes 5767168 | tf_op jit(solution)/shard_map/dot_general | solution.py:93
  185.2 2.3 reshape.231
  187.5 3.3 %copy.47 = bf16[4,64,2,1024]{3,2,0,1:T(2,128)(2,1)} copy(bf16[4,64,2,1024]{3,2,1,0:T(2,128)(2,1)} %reshape.231) | data formatting | bytes 2097152 | tf_op jit(solution)/shard_map/reshape | solution.py:96
  190.9 10.7 %all-to-all-start.3 = ((bf16[64,4,2,1024]{3,2,1,0:T(2,128)(2,1)}), bf16[64,4,2,1024]{3,2,1,0:T(2,128)(2,1)}, u32[]{:S(2)}, u32[]{:S(2)}) async-start(bf16[64,4,2,1024]{3,2,1,0:T(2,128)(2,1)} %bitcast.93), calls=%async_computation.3 | async-start | bytes 2097152 | tf_op jit(solution)/shard_map/all_to_all | solution.py:99
  201.6 3.2 %all-gather.3.cloned.1.call-done = bf16[512,4096]{1,0:T(8,128)(2,1)} async-done(((bf16[128,4096]{1,0:T(8,128)(2,1)}), bf16[512,4096]{1,0:T(8,128)(2,1)}) %all-gather.3.cloned.1.call-update) | async-done | bytes 4194320 | tf_op jit(solution)/shard_map/all_gather | solution.py:88
  204.8 4.7 %fusion.6 = f32[512,384]{1,0:T(8,128)S(1)} fusion(bf16[512,4096]{1,0:T(8,128)(2,1)} %all-gather.3.cloned.1.call-done, bf16[1,4096,384]{2,1,0:T(8,128)(2,1)S(1)} %copy-done), kind=kOutput, calls=%fused_computation.11 | convolution fusion | flops 1610612736 | bytes 8126464 | tf_op jit(solution)/shard_map/dot_general | solution.py:89
  209.5 2.3 fusion.31
  212.5 1.8 collective-permute-start.1
  214.3 0.8 collective-permute-start
  215.1 8.8 %collective-permute-done.2 = bf16[512,384]{1,0:T(8,128)(2,1)S(1)} collective-permute-done((bf16[512,384]{1,0:T(8,128)(2,1)S(1)}, bf16[512,384]{1,0:T(8,128)(2,1)S(1)}, u32[]{:S(2)}, u32[]{:S(2)}) %collective-permute-start.2) | collective-permute-done | bytes 393248 | tf_op jit(solution)/shard_map/ppermute | solution.py:35
  223.9 2.2 collective-permute-done.1
  226.1 7.2 %collective-permute-done = bf16[512,384]{1,0:T(8,128)(2,1)S(1)} collective-permute-done((bf16[512,384]{1,0:T(8,128)(2,1)S(1)}, bf16[512,384]{1,0:T(8,128)(2,1)S(1)}, u32[]{:S(2)}, u32[]{:S(2)}) %collective-permute-start) | collective-permute-done | bytes 393248 | tf_op jit(solution)/shard_map/ppermute | solution.py:35
  233.2 4.4 %bitcast_convert_fusion.1 = bf16[512,1024]{1,0:T(8,128)(2,1)} fusion(bf16[1,512,384]{2,1,0:T(8,128)(2,1)S(1)} %bitcast.105, bf16[1,512,384]{2,1,0:T(8,128)(2,1)S(1)} %bitcast.106, bf16[1,512,384]{2,1,0:T(8,128)(2,1)S(1)} %bitcast.108, bf16[1,512,384]{2,1,0:T(8,128)(2,1)S(1)} %bitcast.103, bf16[1,384,1024]{2,1,0:T(8,128)(2,1)} %bitcast.16, ...), kind=kOutput, calls=%fused_computation.14 | convolution fusion | flops 1618214912 | bytes 5767168 | tf_op jit(solution)/shard_map/dot_general | solution.py:93
  237.7 2.3 reshape.230
  239.9 3.4 %copy.48 = bf16[4,64,2,1024]{3,2,0,1:T(2,128)(2,1)} copy(bf16[4,64,2,1024]{3,2,1,0:T(2,128)(2,1)} %reshape.230) | data formatting | bytes 2097152 | tf_op jit(solution)/shard_map/reshape | solution.py:96
  243.3 10.7 %all-to-all-start.1 = ((bf16[64,4,2,1024]{3,2,1,0:T(2,128)(2,1)}), bf16[64,4,2,1024]{3,2,1,0:T(2,128)(2,1)}, u32[]{:S(2)}, u32[]{:S(2)}) async-start(bf16[64,4,2,1024]{3,2,1,0:T(2,128)(2,1)} %bitcast.92), calls=%async_computation.1 | async-start | bytes 2097152 | tf_op jit(solution)/shard_map/all_to_all | solution.py:99
  254.7 3.5 %convolution_bitcast_fusion = f32[64,1024]{1,0:T(8,128)} fusion(bf16[64,4,2,1024]{3,2,1,0:T(2,128)(2,1)} %all-to-all-done.3, s32[4,2]{1,0:T(4,128)S(1)} %iota_add_fusion, f32[64,64]{1,0:T(8,128)S(1)} %select_reduce_fusion, s32[64,64]{1,0:T(8,128)S(1)} %sub.20, pred[64,64]{1,0:T(8,128)(4,1)S(1)} %broadcast_compare_fusion), kind=kOutput, calls=%fused_computation.33 | convolution fusion | flops 201424896 | bytes 1347616 | tf_op jit(solution)/shard_map/dot_general | solution.py:106
  258.2 24.6 %all-to-all-done.1 = bf16[64,4,2,1024]{3,2,1,0:T(2,128)(2,1)} async-done(((bf16[64,4,2,1024]{3,2,1,0:T(2,128)(2,1)}), bf16[64,4,2,1024]{3,2,1,0:T(2,128)(2,1)}, u32[]{:S(2)}, u32[]{:S(2)}) %all-to-all-start.1) | async-done | bytes 1048608 | tf_op jit(solution)/shard_map/all_to_all | solution.py:99
  282.8 2.8 fusion.35
  286.0 0.9 collective-permute-start.11
  287.0 1.6 collective-permute-start.10
  288.5 1.7 collective-permute-start.9
  290.2 1.0 collective-permute-done.11
  291.2 1.1 collective-permute-done.10
  293.2 0.7 copy.40
  (61 shorter events, 4.2 us)
Async XLA Ops:
  6.5 135.4 %copy-start = (bf16[1,4096,384]{2,1,0:T(8,128)(2,1)S(1)}, bf16[1,4096,384]{2,1,0:T(8,128)(2,1)}, u32[]{:S(2)}) copy-start(bf16[1,4096,384]{2,1,0:T(8,128)(2,1)} %param.15) | copy-start | bytes 9437188
  6.5 135.4 %all-gather.5.cloned.1.call-start = ((), (), s32[]{:S(2)}) async-start(), calls=%async_computation.5 | async-start | bytes 5242880 | tf_op jit(solution)/shard_map/all_gather | solution.py:88
  6.5 9.6 %copy-start.4 = (s32[16,4,8]{0,2,1:T(8,128)S(1)}, s32[16,4,8]{0,2,1:T(8,128)}, u32[]{:S(2)}) copy-start(s32[16,4,8]{0,2,1:T(8,128)} %param.10) | copy-start | bytes 6148
  6.5 10.3 %copy-start.5 = (s32[16]{0:T(128)S(1)}, s32[16]{0:T(128)}, u32[]{:S(2)}) copy-start(s32[16]{0:T(128)} %param.12) | copy-start | bytes 196
  10.3 20.9 %collective-permute-start.3 = (bf16[384,1024]{1,0:T(8,128)(2,1)}, bf16[384,1024]{1,0:T(8,128)(2,1)}, u32[]{:S(2)}, u32[]{:S(2)}) collective-permute-start(bf16[384,1024]{1,0:T(8,128)(2,1)} %get-tuple-element.16), channel_id=1, source_target_pairs={{0,64},{64,128},{128,192},{192,0},{1,65},{65,129},{129,193},{193,1... | collective-permute-start | bytes 2359304 | tf_op jit(solution)/shard_map/ppermute | solution.py:27
  11.9 37.3 %collective-permute-start.4 = (bf16[384,1024]{1,0:T(8,128)(2,1)}, bf16[384,1024]{1,0:T(8,128)(2,1)}, u32[]{:S(2)}, u32[]{:S(2)}) collective-permute-start(bf16[384,1024]{1,0:T(8,128)(2,1)} %get-tuple-element.18), channel_id=1, source_target_pairs={{0,128},{64,192},{128,0},{192,64},{1,129},{65,193},{129,1},{193,65... | collective-permute-start | bytes 2359304 | tf_op jit(solution)/shard_map/ppermute | solution.py:27
  14.8 34.4 %collective-permute-start.5 = (bf16[384,1024]{1,0:T(8,128)(2,1)}, bf16[384,1024]{1,0:T(8,128)(2,1)}, u32[]{:S(2)}, u32[]{:S(2)}) collective-permute-start(bf16[384,1024]{1,0:T(8,128)(2,1)} %get-tuple-element.15), channel_id=1, source_target_pairs={{0,192},{64,0},{128,64},{192,128},{1,193},{65,1},{129,65},{193,129... | collective-permute-start | bytes 2359304 | tf_op jit(solution)/shard_map/ppermute | solution.py:27
  95.0 109.8 %all-gather.3.cloned.1.call-start = ((), (), s32[]{:S(2)}) async-start(), calls=%async_computation.4 | async-start | bytes 5242880 | tf_op jit(solution)/shard_map/all_gather | solution.py:88
  141.9 4.7 %copy-start.7 = (bf16[512,4096]{1,0:T(8,128)(2,1)S(1)}, bf16[512,4096]{1,0:T(8,128)(2,1)}, u32[]{:S(2)}) copy-start(bf16[512,4096]{1,0:T(8,128)(2,1)} %all-gather.5.cloned.1.call-done) | copy-start | bytes 12582916
  141.9 4.7 %copy-start.8 = (bf16[1,4096,384]{2,1,0:T(8,128)(2,1)S(1)}, bf16[1,4096,384]{2,1,0:T(8,128)(2,1)}, u32[]{:S(2)}) copy-start(bf16[1,4096,384]{2,1,0:T(8,128)(2,1)} %param.16) | copy-start | bytes 9437188
  146.6 34.1 %copy-start.1 = (bf16[384,1024]{1,0:T(8,128)(2,1)S(1)}, bf16[384,1024]{1,0:T(8,128)(2,1)}, u32[]{:S(2)}) copy-start(bf16[384,1024]{1,0:T(8,128)(2,1)} %get-tuple-element.10) | copy-start | bytes 2359300
  149.0 12.8 %collective-permute-start.8 = (bf16[512,384]{1,0:T(8,128)(2,1)S(1)}, bf16[512,384]{1,0:T(8,128)(2,1)S(1)}, u32[]{:S(2)}, u32[]{:S(2)}) collective-permute-start(bf16[512,384]{1,0:T(8,128)(2,1)S(1)} %fusion.28), channel_id=1, source_target_pairs={{0,192},{64,0},{128,64},{192,128},{1,193},{65,1},{129,65},{193,129... | collective-permute-start | bytes 1179656 | tf_op jit(solution)/shard_map/ppermute | solution.py:35
  150.2 16.1 %collective-permute-start.7 = (bf16[512,384]{1,0:T(8,128)(2,1)S(1)}, bf16[512,384]{1,0:T(8,128)(2,1)S(1)}, u32[]{:S(2)}, u32[]{:S(2)}) collective-permute-start(bf16[512,384]{1,0:T(8,128)(2,1)S(1)} %fusion.28), channel_id=1, source_target_pairs={{0,128},{64,192},{128,0},{192,64},{1,129},{65,193},{129,1},{193,65... | collective-permute-start | bytes 1179656 | tf_op jit(solution)/shard_map/ppermute | solution.py:35
  152.0 28.7 %collective-permute-start.6 = (bf16[512,384]{1,0:T(8,128)(2,1)S(1)}, bf16[512,384]{1,0:T(8,128)(2,1)S(1)}, u32[]{:S(2)}, u32[]{:S(2)}) collective-permute-start(bf16[512,384]{1,0:T(8,128)(2,1)S(1)} %fusion.28), channel_id=1, source_target_pairs={{0,64},{64,128},{128,192},{192,0},{1,65},{65,129},{129,193},{193,1... | collective-permute-start | bytes 1179656 | tf_op jit(solution)/shard_map/ppermute | solution.py:35
  190.9 52.5 %all-to-all-start.3 = ((bf16[64,4,2,1024]{3,2,1,0:T(2,128)(2,1)}), bf16[64,4,2,1024]{3,2,1,0:T(2,128)(2,1)}, u32[]{:S(2)}, u32[]{:S(2)}) async-start(bf16[64,4,2,1024]{3,2,1,0:T(2,128)(2,1)} %bitcast.93), calls=%async_computation.3 | async-start | bytes 2097152 | tf_op jit(solution)/shard_map/all_to_all | solution.py:99
  204.8 4.7 %copy-start.6 = (bf16[512,4096]{1,0:T(8,128)(2,1)S(1)}, bf16[512,4096]{1,0:T(8,128)(2,1)}, u32[]{:S(2)}) copy-start(bf16[512,4096]{1,0:T(8,128)(2,1)} %all-gather.3.cloned.1.call-done) | copy-start | bytes 12582916
  204.8 4.7 %copy-start.9 = (bf16[1,4096,384]{2,1,0:T(8,128)(2,1)S(1)}, bf16[1,4096,384]{2,1,0:T(8,128)(2,1)}, u32[]{:S(2)}) copy-start(bf16[1,4096,384]{2,1,0:T(8,128)(2,1)} %param.16) | copy-start | bytes 9437188
  209.5 23.8 %copy-start.2 = (bf16[384,1024]{1,0:T(8,128)(2,1)S(1)}, bf16[384,1024]{1,0:T(8,128)(2,1)}, u32[]{:S(2)}) copy-start(bf16[384,1024]{1,0:T(8,128)(2,1)} %get-tuple-element.10) | copy-start | bytes 2359300
  211.8 12.1 %collective-permute-start.2 = (bf16[512,384]{1,0:T(8,128)(2,1)S(1)}, bf16[512,384]{1,0:T(8,128)(2,1)S(1)}, u32[]{:S(2)}, u32[]{:S(2)}) collective-permute-start(bf16[512,384]{1,0:T(8,128)(2,1)S(1)} %fusion.31), channel_id=1, source_target_pairs={{0,192},{64,0},{128,64},{192,128},{1,193},{65,1},{129,65},{193,129... | collective-permute-start | bytes 1179656 | tf_op jit(solution)/shard_map/ppermute | solution.py:35
  212.5 13.6 %collective-permute-start.1 = (bf16[512,384]{1,0:T(8,128)(2,1)S(1)}, bf16[512,384]{1,0:T(8,128)(2,1)S(1)}, u32[]{:S(2)}, u32[]{:S(2)}) collective-permute-start(bf16[512,384]{1,0:T(8,128)(2,1)S(1)} %fusion.31), channel_id=1, source_target_pairs={{0,128},{64,192},{128,0},{192,64},{1,129},{65,193},{129,1},{193,65... | collective-permute-start | bytes 1179656 | tf_op jit(solution)/shard_map/ppermute | solution.py:35
  214.3 18.9 %collective-permute-start = (bf16[512,384]{1,0:T(8,128)(2,1)S(1)}, bf16[512,384]{1,0:T(8,128)(2,1)S(1)}, u32[]{:S(2)}, u32[]{:S(2)}) collective-permute-start(bf16[512,384]{1,0:T(8,128)(2,1)S(1)} %fusion.31), channel_id=1, source_target_pairs={{0,64},{64,128},{128,192},{192,0},{1,65},{65,129},{129,193},{193,1... | collective-permute-start | bytes 1179656 | tf_op jit(solution)/shard_map/ppermute | solution.py:35
  237.7 16.4 %copy-start.3 = (f32[16,4,8]{0,2,1:T(8,128)S(1)}, f32[16,4,8]{0,2,1:T(8,128)}, u32[]{:S(2)}) copy-start(f32[16,4,8]{0,2,1:T(8,128)} %param.11) | copy-start | bytes 6148
  237.7 16.8 %copy-start.10 = (s32[16]{0:T(128)S(1)}, s32[16]{0:T(128)}, u32[]{:S(2)}) copy-start(s32[16]{0:T(128)} %param.14) | copy-start | bytes 196
  243.3 39.5 %all-to-all-start.1 = ((bf16[64,4,2,1024]{3,2,1,0:T(2,128)(2,1)}), bf16[64,4,2,1024]{3,2,1,0:T(2,128)(2,1)}, u32[]{:S(2)}, u32[]{:S(2)}) async-start(bf16[64,4,2,1024]{3,2,1,0:T(2,128)(2,1)} %bitcast.92), calls=%async_computation.1 | async-start | bytes 2097152 | tf_op jit(solution)/shard_map/all_to_all | solution.py:99
  286.0 5.2 %collective-permute-start.11 = (bf16[1,4,4,1024]{3,2,1,0:T(4,128)(2,1)S(1)}, bf16[1,4,4,1024]{3,2,1,0:T(4,128)(2,1)S(1)}, u32[]{:S(2)}, u32[]{:S(2)}) collective-permute-start(bf16[1,4,4,1024]{3,2,1,0:T(4,128)(2,1)S(1)} %get-tuple-element.20), channel_id=1, source_target_pairs={{0,192},{64,128},{128,64},{192,0},{1,193},{65,129},{129,65},{193,1... | collective-permute-start | bytes 98312 | tf_op jit(solution)/shard_map/ppermute | solution.py:131
  287.0 5.4 %collective-permute-start.10 = (bf16[1,4,4,1024]{3,2,1,0:T(4,128)(2,1)S(1)}, bf16[1,4,4,1024]{3,2,1,0:T(4,128)(2,1)S(1)}, u32[]{:S(2)}, u32[]{:S(2)}) collective-permute-start(bf16[1,4,4,1024]{3,2,1,0:T(4,128)(2,1)S(1)} %get-tuple-element.21), channel_id=1, source_target_pairs={{0,128},{64,192},{128,0},{192,64},{1,129},{65,193},{129,1},{193,65... | collective-permute-start | bytes 98312 | tf_op jit(solution)/shard_map/ppermute | solution.py:131
  288.5 3.9 %collective-permute-start.9 = (bf16[1,4,4,1024]{3,2,1,0:T(4,128)(2,1)S(1)}, bf16[1,4,4,1024]{3,2,1,0:T(4,128)(2,1)S(1)}, u32[]{:S(2)}, u32[]{:S(2)}) collective-permute-start(bf16[1,4,4,1024]{3,2,1,0:T(4,128)(2,1)S(1)} %get-tuple-element.22), channel_id=1, source_target_pairs={{0,64},{64,0},{128,192},{192,128},{1,65},{65,1},{129,193},{193,129... | collective-permute-start | bytes 98312 | tf_op jit(solution)/shard_map/ppermute | solution.py:131
Sparse Core Ops, SparseCore 0:
  95.1 46.8 all-gather.4
  143.7 60.9 all-gather.2
